TPU v7x, 512 devices: a whole 4x8x8 slice. The times are simulated.
512 devices in a mesh: dp: 16 (over z_hi, y), tensor: 32 (over x, z_lo, core).
Axes of the slice: x: 4, y: 8, z: 8 (z_hi: 2, z_lo: 4; z = z_hi * 4 + z_lo), core: 2. Of those that a mesh axis runs over, the one named last changes fastest.
Arguments:
- suffix_states: bfloat16 [32, 128, 2048], P(None, 'dp', 'tensor'), may hold values from -16 to 16
- suffix_lengths: int32 [32], replicated, may hold values from 1 to 128, 2560 in all
- request_group: int32 [32, 1], replicated, may hold values from 0 to 15
- group_owner: int32 [16], replicated, may hold values from 0 to 15, each once
- request_order: int32 [32], replicated, may hold values from 0 to 31, each once
- prefix_cache: bfloat16 [16, 256, 1024], P('dp', 'tensor'), may hold values from -700 to 700
- norm_attn: bfloat16 [2048], replicated, may hold values from 0.099609375 to 1.8984375
- w_query: bfloat16 [2048, 2048], P(None, 'tensor'), may hold values from -0.125 to 0.125
- w_key: bfloat16 [2048, 512], P(None, 'tensor'), may hold values from -0.125 to 0.125
- w_value: bfloat16 [2048, 512], P(None, 'tensor'), may hold values from -0.125 to 0.125
- w_out: bfloat16 [2048, 2048], P('tensor'), may hold values from -0.25 to 0.25
- norm_mlp: bfloat16 [2048], replicated, may hold values from 0.099609375 to 1.8984375
- w_gate: bfloat16 [2048, 8192], P(None, 'tensor'), may hold values from -0.125 to 0.125
- w_up: bfloat16 [2048, 8192], P(None, 'tensor'), may hold values from -0.125 to 0.125
- w_down: bfloat16 [8192, 2048], P('tensor'), may hold values from -0.125 to 0.125
Outputs:
- hidden_out: bfloat16 [32, 128, 2048], P(None, 'dp', 'tensor')
- suffix_keys: bfloat16 [32, 128, 512], P('dp', None, 'tensor')
- suffix_values: bfloat16 [32, 128, 512], P('dp', None, 'tensor')
Inputs may be any that keep to these rules, and one draw needn't show every extreme that they name: `suffix_lengths`: the lengths sum to 2560 and some request has exactly 128. `request_group`: every group has at least one request. `group_owner`: A permutation of the 16 groups onto the slots of prefix_cache. `request_order`: A permutation of the requests; slot s belongs to index s // 2 of dp.
All inputs are finite; a program needn't handle non-finite values.
Results may differ from a plain program's by a relative error of at most 0.03.
Values may be sent and summed in bfloat16 or wider, within the bound.
No kernel may reach another device: no remote copies, remote signals or barrier semaphores. Data moves between devices by JAX's collectives and lax.ppermute only.
A program may use at most 64 MiB of HBM per device.

v0:
```python
import jax
import jax.numpy as jnp
import numpy as np
from jax import lax
from jax.sharding import PartitionSpec as P

H = 32
KVH = 8
HD = 64
L_MAX = 128
P_SIZE = 256
THETA = 10000000.0
EPSILON = 1e-05


def rms_scale(states, gain):
    wide = states.astype(jnp.float32)
    mean_square = jnp.mean(wide * wide, axis=-1, keepdims=True)
    return (wide * lax.rsqrt(mean_square + EPSILON) * gain.astype(jnp.float32)).astype(jnp.bfloat16)


def rotate(vectors, positions):
    half = HD // 2
    freqs = THETA ** (-(jnp.arange(half, dtype=jnp.float32) * 2.0 / HD))
    angles = positions[:, None] * freqs[None, :]
    cosine = jnp.cos(angles)[:, None, :]
    sine = jnp.sin(angles)[:, None, :]
    first = vectors[..., :half]
    second = vectors[..., half:]
    return jnp.concatenate(
        [first * cosine - second * sine, second * cosine + first * sine], axis=-1
    )


def absorb_block(state_now, scores, allowed, value_rows):
    running_max, running_sum, numerator = state_now
    block_max = jnp.max(jnp.where(allowed, scores, -1e30), axis=2)
    new_max = jnp.maximum(running_max, block_max)
    rescale = jnp.exp(running_max - new_max)
    weights = jnp.where(allowed, jnp.exp(scores - new_max[:, :, None]), 0.0)
    running_sum = running_sum * rescale + jnp.sum(weights, axis=2)
    numerator = numerator * rescale[:, :, None] + jnp.einsum(
        "htk,khd->htd", weights.astype(jnp.bfloat16), value_rows, preferred_element_type=jnp.float32
    )
    return (new_max, running_sum, numerator)


def shards(
    suffix_states,
    suffix_lengths,
    request_group,
    group_owner,
    request_order,
    prefix_cache,
    norm_attn,
    w_query,
    w_key,
    w_value,
    w_out,
    norm_mlp,
    w_gate,
    w_up,
    w_down,
):
    dp_count = lax.axis_size("dp")
    tp_count = lax.axis_size("tensor")
    dp_index = lax.axis_index("dp")
    tp_index = lax.axis_index("tensor")
    total_reqs = suffix_lengths.shape[0]
    local_reqs = total_reqs // dp_count
    row_count = local_reqs * L_MAX
    heads_here = w_query.shape[1] // HD
    group_size = H // KVH
    kv_here = max(1, heads_here // group_size)
    slab_width = kv_here * 2 * HD
    score_scale = HD ** (-0.5)
    head_map = np.arange(heads_here) // group_size
    dest_table = (
        np.arange(tp_count)[:, None] * heads_here // group_size + np.arange(kv_here)[None, :]
    ).reshape(-1)
    routed = jnp.take(suffix_states, request_order, axis=0)
    routed_here = lax.all_to_all(routed, "dp", split_axis=0, concat_axis=1, tiled=True)
    width_here = routed_here.shape[2]
    state_shard = routed_here.reshape(row_count, width_here)
    slot_ids = dp_index * local_reqs + jnp.arange(local_reqs, dtype=jnp.int32)
    req_ids = jnp.take(request_order, slot_ids)
    lengths_here = jnp.take(suffix_lengths, req_ids)
    owner_here = jnp.take(group_owner, jnp.take(request_group[:, 0], req_ids))
    position = jnp.arange(L_MAX, dtype=jnp.int32)
    valid = (position[None, :] < lengths_here[:, None]).reshape(row_count)
    positions = (P_SIZE + jnp.tile(position, local_reqs)).astype(jnp.float32)
    full_rows = lax.all_gather(state_shard, "tensor", axis=1, tiled=True)
    normed = rms_scale(full_rows, norm_attn)
    query = rotate(
        jnp.dot(normed, w_query, preferred_element_type=jnp.float32).reshape(
            row_count, heads_here, HD
        ),
        positions,
    ).astype(jnp.bfloat16)
    key_part = jnp.dot(normed, w_key, preferred_element_type=jnp.float32).astype(jnp.bfloat16)
    value_part = jnp.dot(normed, w_value, preferred_element_type=jnp.float32).astype(jnp.bfloat16)
    key_full, value_full = (
        lax.all_gather(key_part, "tensor", axis=1, tiled=True),
        lax.all_gather(value_part, "tensor", axis=1, tiled=True),
    )
    key_heads = key_full.reshape(row_count, HD, KVH).transpose(0, 2, 1)
    value_heads = value_full.reshape(row_count, HD, KVH).transpose(0, 2, 1)
    key_rot = rotate(key_heads.astype(jnp.float32), positions).astype(jnp.bfloat16)
    cache_width = key_part.shape[1]
    keys_flat = jnp.where(valid[:, None], key_rot.reshape(row_count, KVH * HD), 0.0)
    values_flat = jnp.where(valid[:, None], value_heads.reshape(row_count, KVH * HD), 0.0)
    keys_out = lax.dynamic_slice_in_dim(keys_flat, tp_index * cache_width, cache_width, 1).reshape(
        local_reqs, L_MAX, cache_width
    )
    values_out = lax.dynamic_slice_in_dim(
        values_flat, tp_index * cache_width, cache_width, 1
    ).reshape(local_reqs, L_MAX, cache_width)
    kv_first = tp_index * heads_here // group_size
    own_keys = lax.dynamic_slice_in_dim(key_rot, kv_first, kv_here, 1)[:, head_map].reshape(
        local_reqs, L_MAX, heads_here, HD
    )
    own_values = lax.dynamic_slice_in_dim(value_heads, kv_first, kv_here, 1)[:, head_map].reshape(
        local_reqs, L_MAX, heads_here, HD
    )
    query_req = query.reshape(local_reqs, L_MAX, heads_here, HD)

    def absorb_prefix(state_one, query_one, slot_block):
        block = slot_block.reshape(slot_block.shape[0], kv_here, 2, HD)
        key_rows = block[:, head_map, 0]
        value_rows = block[:, head_map, 1]
        scores = (
            jnp.einsum("thd,phd->htp", query_one, key_rows, preferred_element_type=jnp.float32)
            * score_scale
        )
        return absorb_block(state_one, scores, jnp.ones((1, 1, 1), bool), value_rows)

    initial = tuple(
        (
            (
                jnp.full((heads_here, L_MAX), -1e30, jnp.float32),
                jnp.zeros((heads_here, L_MAX), jnp.float32),
                jnp.zeros((heads_here, L_MAX, HD), jnp.float32),
            )
            for request in range(local_reqs)
        )
    )
    all_rows = lax.all_gather(prefix_cache, "dp", axis=0, tiled=True)
    rows_each = all_rows.shape[1]
    chosen = jnp.take(all_rows.reshape(dp_count, rows_each, KVH, 2 * HD), dest_table, axis=2)
    picked = lax.all_to_all(chosen, "tensor", split_axis=2, concat_axis=1, tiled=True).reshape(
        dp_count, P_SIZE, slab_width
    )
    states = tuple(
        (
            absorb_prefix(
                initial[request],
                query_req[request],
                lax.dynamic_index_in_dim(picked, owner_here[request], 0, keepdims=False),
            )
            for request in range(local_reqs)
        )
    )
    pieces = []
    for request in range(local_reqs):
        self_scores = (
            jnp.einsum(
                "thd,shd->hts",
                query_req[request],
                own_keys[request],
                preferred_element_type=jnp.float32,
            )
            * score_scale
        )
        self_allowed = (position[None, :] <= position[:, None]) & (
            position[None, :] < lengths_here[request]
        )
        running_max, running_sum, numerator = absorb_block(
            states[request], self_scores, self_allowed[None], own_values[request]
        )
        attention_one = (numerator / running_sum[:, :, None]).astype(jnp.bfloat16)
        pieces.append(attention_one.transpose(1, 0, 2).reshape(L_MAX, heads_here * HD))
    attention = jnp.concatenate(pieces, axis=0)
    attn_terms = jnp.dot(attention, w_out, preferred_element_type=jnp.float32)
    attn_share = lax.psum_scatter(
        attn_terms.astype(jnp.bfloat16), "tensor", scatter_dimension=1, tiled=True
    ).astype(jnp.float32)
    middle = (state_shard.astype(jnp.float32) + attn_share).astype(jnp.bfloat16)
    middle_rows = lax.all_gather(middle, "tensor", axis=1, tiled=True)
    normed_two = rms_scale(middle_rows, norm_mlp)
    gate = jnp.dot(normed_two, w_gate, preferred_element_type=jnp.float32)
    upper = jnp.dot(normed_two, w_up, preferred_element_type=jnp.float32)
    hidden = (jax.nn.silu(gate) * upper).astype(jnp.bfloat16)
    down_terms = jnp.dot(hidden, w_down, preferred_element_type=jnp.float32)
    down_share = lax.psum_scatter(
        down_terms.astype(jnp.bfloat16), "tensor", scatter_dimension=1, tiled=True
    ).astype(jnp.float32)
    result = middle.astype(jnp.float32) + down_share
    result = (
        jnp.where(valid[:, None], result, 0.0)
        .astype(jnp.bfloat16)
        .reshape(local_reqs, L_MAX, width_here)
    )
    returned = lax.all_to_all(result, "dp", split_axis=1, concat_axis=0, tiled=True)
    hidden_out = jnp.zeros_like(returned).at[request_order].set(returned)
    return (hidden_out, keys_out, values_out)


def solution(mesh):
    in_specs = (
        P(None, "dp", "tensor"),
        P(),
        P(),
        P(),
        P(),
        P("dp", "tensor", None),
        P(),
        P(None, "tensor"),
        P(None, "tensor"),
        P(None, "tensor"),
        P("tensor", None),
        P(),
        P(None, "tensor"),
        P(None, "tensor"),
        P("tensor", None),
    )
    out_specs = (P(None, "dp", "tensor"), P("dp", None, "tensor"), P("dp", None, "tensor"))
    return jax.shard_map(shards, mesh=mesh, in_specs=in_specs, out_specs=out_specs, check_vma=False)
```

profile of v0, /device:TPU:8, one launch (start us, length us, event | category | flops | bytes accessed | tf_op | source)
XLA Modules:
  0.0 635.4 jit_solution(12212164289237570744)
XLA Ops:
  7.2 0.7 compare_select_fusion.3
  7.9 0.7 compare_and_fusion.1
  8.6 1.4 gather_fusion
  10.0 0.1 broadcast_select_fusion
  10.1 0.7 reshape.707
  10.9 16.0 %all-to-all-start = ((bf16[16,2,512]{2,1,0:T(2,128)(2,1)}), bf16[16,2,512]{2,1,0:T(2,128)(2,1)S(1)}, u32[]{:S(2)}, u32[]{:S(2)}) async-start(bf16[16,2,512]{2,1,0:T(2,128)(2,1)} %reshape.707), calls=%async_computation | async-start | bytes 65536 | tf_op jit(solution)/shard_map/all_to_all | solution.py:82
  26.9 49.1 %all_gather.16 = bf16[16,8,1024]{2,1,0:T(8,128)(2,1)S(1)} all-gather(bf16[1,8,1024]{2,1,0:T(8,128)(2,1)} %param.30), channel_id=1, replica_groups=mesh['dp'=16,'tensor'=32] {'dp'}, dimensions={0}, use_global_device_ids=true | all-gather | bytes 278528 | tf_op jit(solution)/shard_map/all_gather | solution.py:147
  76.0 0.7 pad_clamp_fusion.1
  76.7 1.9 gather_fusion.1
  78.6 6.7 %all-to-all-start.1 = ((bf16[16,8,32,128]{3,1,0,2:T(8,128)(2,1)}), bf16[16,8,32,128]{3,1,0,2:T(8,128)(2,1)S(1)}, u32[]{:S(2)}, u32[]{:S(2)}) async-start(bf16[16,8,32,128]{3,1,0,2:T(8,128)(2,1)} %bitcast.9), calls=%async_computation.1 | async-start | bytes 2097152 | tf_op jit(solution)/shard_map/all_to_all | solution.py:150
  85.4 0.6 gather_fusion.3
  86.0 0.1 reshape.708
  86.1 0.7 copy.51
  87.0 0.6 gather_fusion.5
  87.6 0.6 gather_fusion.4
  88.3 0.6 gather_fusion.2
  88.9 0.6 fusion.81
  93.5 0.6 fusion.80
  94.1 0.6 iota_compare_fusion.2
  94.7 0.7 iota_compare_fusion.1
  95.4 0.2 multiply_cosine_fusion
  95.6 17.5 %all-to-all-done.1 = bf16[16,8,32,128]{3,1,0,2:T(8,128)(2,1)S(1)} async-done(((bf16[16,8,32,128]{3,1,0,2:T(8,128)(2,1)}), bf16[16,8,32,128]{3,1,0,2:T(8,128)(2,1)S(1)}, u32[]{:S(2)}, u32[]{:S(2)}) %all-to-all-start.1) | async-done | bytes 1048608 | tf_op jit(solution)/shard_map/all_to_all | solution.py:150
  113.1 0.3 copy_bitcast_fusion
  113.4 0.1 copy.54
  113.5 0.1 copy.57
  113.6 37.2 %all-gather.3.cloned.1.call-done = bf16[256,2048]{0,1:T(8,128)(2,1)} async-done(((bf16[256,64]{0,1:T(8,128)(2,1)}), bf16[256,2048]{0,1:T(8,128)(2,1)}) %all-gather.3.cloned.1.call-update) | async-done | bytes 1048592 | tf_op jit(solution)/shard_map/all_gather | solution.py:92
  150.8 1.6 fusion
  152.5 0.5 convolution_bitcast_fusion
  153.0 0.2 fusion.42
  153.2 0.1 copy-done.14
  153.3 0.5 convolution_convert_fusion.2
  153.8 41.5 %all_gather.18 = bf16[256,512]{0,1:T(8,128)(2,1)S(1)} all-gather(bf16[256,16]{0,1:T(8,128)(2,1)S(1)} %convolution_convert_fusion.2), channel_id=1, replica_groups=mesh['dp'=16,'tensor'=32] {'tensor'}, dimensions={1}, use_global_device_ids=true | all-gather | bytes 270336 | tf_op jit(solution)/shard_map/all_gather | solution.py:104
  195.4 0.5 convolution_convert_fusion.3
  195.8 38.9 %all_gather.17 = bf16[256,512]{0,1:T(8,128)(2,1)S(1)} all-gather(bf16[256,16]{0,1:T(8,128)(2,1)S(1)} %convolution_convert_fusion.3), channel_id=1, replica_groups=mesh['dp'=16,'tensor'=32] {'tensor'}, dimensions={1}, use_global_device_ids=true | all-gather | bytes 270336 | tf_op jit(solution)/shard_map/all_gather | solution.py:103
  234.8 0.2 copy.71
  235.0 0.3 fusion.82
  235.2 0.3 fusion.83
  235.7 0.2 select_reduce_fusion.1
  235.9 0.2 select_reduce_fusion
  236.1 0.1 fusion.35
  236.2 0.2 fusion.25
  236.5 0.2 fusion.9
  236.7 0.1 fusion.33
  236.8 0.2 fusion.23
  237.0 0.2 fusion.10
  237.2 0.2 fusion.12
  237.5 0.2 fusion.11
  237.7 1.5 convolution_convert_fusion.1
  239.2 147.1 %reduce-scatter.3.cloned.1.call-done = bf16[256,64]{0,1:T(8,128)(2,1)} async-done(((bf16[256,2048]{0,1:T(8,128)(2,1)}), bf16[256,64]{0,1:T(8,128)(2,1)}) %reduce-scatter.3.cloned.1.call-update) | async-done | bytes 32784 | tf_op jit(solution)/shard_map/reduce_scatter | solution.py:184
  386.3 1.4 add_convert_fusion
  387.8 59.3 %all-gather.5.cloned.1.call-done = bf16[256,2048]{0,1:T(8,128)(2,1)} async-done(((bf16[256,64]{0,1:T(8,128)(2,1)}), bf16[256,2048]{0,1:T(8,128)(2,1)}) %all-gather.5.cloned.1.call-update) | async-done | bytes 1048592 | tf_op jit(solution)/shard_map/all_gather | solution.py:188
  447.1 1.6 fusion.3
  448.8 2.1 fusion.15
  450.9 4.1 convolution_convert_fusion
  455.1 148.5 %reduce-scatter.5.cloned.1.call-done = bf16[256,64]{0,1:T(8,128)(2,1)} async-done(((bf16[256,2048]{0,1:T(8,128)(2,1)}), bf16[256,64]{0,1:T(8,128)(2,1)}) %reduce-scatter.5.cloned.1.call-update) | async-done | bytes 32784 | tf_op jit(solution)/shard_map/reduce_scatter | solution.py:194
  603.6 0.8 select_convert_fusion
  604.4 0.1 copy.58
  604.5 0.7 reshape.709
  605.2 10.2 %all-to-all-start.2 = ((bf16[16,2,512]{2,1,0:T(2,128)(2,1)}), bf16[16,2,512]{2,1,0:T(2,128)(2,1)S(1)}, u32[]{:S(2)}, u32[]{:S(2)}) async-start(bf16[16,2,512]{2,1,0:T(2,128)(2,1)} %reshape.709), calls=%async_computation.4 | async-start | bytes 65536 | tf_op jit(solution)/shard_map/all_to_all | solution.py:203
  615.4 0.6 copy_bitcast_fusion.3
  616.0 10.5 %all-to-all-done.2 = bf16[16,2,512]{2,1,0:T(2,128)(2,1)S(1)} async-done(((bf16[16,2,512]{2,1,0:T(2,128)(2,1)}), bf16[16,2,512]{2,1,0:T(2,128)(2,1)S(1)}, u32[]{:S(2)}, u32[]{:S(2)}) %all-to-all-start.2) | async-done | bytes 32800 | tf_op jit(solution)/shard_map/all_to_all | solution.py:203
  626.6 0.1 reshape.710
  626.8 1.5 scatter_fusion
  628.3 0.6 copy-done.9
  (69 shorter events, 0.8 us)
Async XLA Ops:
  7.2 443.7 %copy-start = (bf16[256,2048]{1,0:T(8,128)(2,1)S(1)}, bf16[256,2048]{1,0:T(8,128)(2,1)}, u32[]{:S(2)}) copy-start(bf16[256,2048]{1,0:T(8,128)(2,1)} %param.39) | copy-start | bytes 3145732
  10.9 67.7 %all-to-all-start = ((bf16[16,2,512]{2,1,0:T(2,128)(2,1)}), bf16[16,2,512]{2,1,0:T(2,128)(2,1)S(1)}, u32[]{:S(2)}, u32[]{:S(2)}) async-start(bf16[16,2,512]{2,1,0:T(2,128)(2,1)} %reshape.707), calls=%async_computation | async-start | bytes 65536 | tf_op jit(solution)/shard_map/all_to_all | solution.py:82
  78.6 6.8 %copy-start.1 = (s32[32]{0:T(128)S(1)}, s32[32]{0:T(128)}, u32[]{:S(2)}) copy-start(s32[32]{0:T(128)} %param.29) | copy-start | bytes 388
  78.6 8.4 %copy-start.2 = (s32[32,1]{0,1:T(1,128)S(1)}, s32[32,1]{0,1:T(1,128)}, u32[]{:S(2)}) copy-start(s32[32,1]{0,1:T(1,128)} %param.27) | copy-start | bytes 388
  78.6 34.5 %all-to-all-start.1 = ((bf16[16,8,32,128]{3,1,0,2:T(8,128)(2,1)}), bf16[16,8,32,128]{3,1,0,2:T(8,128)(2,1)S(1)}, u32[]{:S(2)}, u32[]{:S(2)}) async-start(bf16[16,8,32,128]{3,1,0,2:T(8,128)(2,1)} %bitcast.9), calls=%async_computation.1 | async-start | bytes 2097152 | tf_op jit(solution)/shard_map/all_to_all | solution.py:150
  85.3 2.4 copy-start.3
  85.3 3.0 copy-start.4
  85.3 65.6 %all-gather.3.cloned.1.call-start = ((), (), s32[]{:S(2)}) async-start(), calls=%async_computation.5 | async-start | bytes 1081344 | tf_op jit(solution)/shard_map/all_gather | solution.py:92
  86.0 6.1 copy-start.11
  86.9 299.5 %reduce-scatter.3.cloned.1.call-start = ((), (), s32[]{:S(2)}) async-start(), calls=%async_computation.6 | async-start | bytes 1081344 | tf_op jit(solution)/shard_map/reduce_scatter | solution.py:184
  113.4 39.1 %copy-start.13 = (bf16[2048,64]{0,1:T(8,128)(2,1)S(1)}, bf16[2048,64]{0,1:T(8,128)(2,1)}, u32[]{:S(2)}) copy-start(bf16[2048,64]{0,1:T(8,128)(2,1)} %param.32) | copy-start | bytes 786436
  150.8 1.6 copy-start.5
  152.5 0.8 copy-start.14
  153.3 42.0 %copy-start.15 = (bf16[2048,16]{0,1:T(8,128)(2,1)S(1)}, bf16[2048,16]{0,1:T(8,128)(2,1)}, u32[]{:S(2)}) copy-start(bf16[2048,16]{0,1:T(8,128)(2,1)} %param.33) | copy-start | bytes 196612
  235.6 2.1 copy-start.10
  237.7 148.7 %copy-start.7 = (bf16[256,64]{0,1:T(8,128)(2,1)S(1)}, bf16[256,64]{0,1:T(8,128)(2,1)}, u32[]{:S(2)}) copy-start(bf16[256,64]{0,1:T(8,128)(2,1)} %copy.51) | copy-start | bytes 98308
  237.7 150.1 %copy-start.12 = (bf16[2048]{0:T(1024)(128)(2,1)S(1)}, bf16[2048]{0:T(1024)(128)(2,1)}, u32[]{:S(2)}) copy-start(bf16[2048]{0:T(1024)(128)(2,1)} %param.36) | copy-start | bytes 12292
  239.2 207.9 %all-gather.5.cloned.1.call-start = ((), (), s32[]{:S(2)}) async-start(), calls=%async_computation.7 | async-start | bytes 1081344 | tf_op jit(solution)/shard_map/all_gather | solution.py:188
  387.7 215.8 %reduce-scatter.5.cloned.1.call-start = ((), (), s32[]{:S(2)}) async-start(), calls=%async_computation.8 | async-start | bytes 1081344 | tf_op jit(solution)/shard_map/reduce_scatter | solution.py:194
  447.1 1.6 copy-start.6
  454.9 148.7 %copy-start.8 = (bf16[256,64]{0,1:T(8,128)(2,1)S(1)}, bf16[256,64]{0,1:T(8,128)(2,1)}, u32[]{:S(2)}) copy-start(bf16[256,64]{0,1:T(8,128)(2,1)} %add_convert_fusion) | copy-start | bytes 98308
  605.2 21.4 %all-to-all-start.2 = ((bf16[16,2,512]{2,1,0:T(2,128)(2,1)}), bf16[16,2,512]{2,1,0:T(2,128)(2,1)S(1)}, u32[]{:S(2)}, u32[]{:S(2)}) async-start(bf16[16,2,512]{2,1,0:T(2,128)(2,1)} %reshape.709), calls=%async_computation.4 | async-start | bytes 65536 | tf_op jit(solution)/shard_map/all_to_all | solution.py:203
  628.3 0.6 copy-start.9
Sparse Core Ops, SparseCore 0:
  88.8 61.9 all-gather.2
  239.3 146.9 reduce-scatter.2
  389.1 58.0 all-gather.4
  455.1 148.4 reduce-scatter.4
where the time goes:
time: 636 us; the launch traced here: 635 us
  waiting for transfers between devices  420 us (66%)
  blocking collectives  130 us (20%)
  starting transfers between devices  33.1 us (5%)
  between operations  18.1 us (3%)
  local copies, waits for them, and re-layouts  13.2 us (2%)
  matrix products  11 us (2%)
  other arithmetic  10.2 us (2%)
    reduce_scatter x1, waiting for transfers between devices, shards(): lax.psum_scatter(down_terms.astype(jnp.bfloat16), 'tensor', scatter_dimen...  149 us
    reduce_scatter x1, waiting for transfers between devices, shards(): lax.psum_scatter(attn_terms.astype(jnp.bfloat16), 'tensor', scatter_dimen...  147 us
    all_gather x1, waiting for transfers between devices, shards(): middle_rows = lax.all_gather(middle, 'tensor', axis=1, tiled=True)  59.3 us
    all_gather x1, blocking collectives, shards(): all_rows = lax.all_gather(prefix_cache, 'dp', axis=0, tiled=True)  49.1 us
    all_gather x1, blocking collectives, shards(): lax.all_gather(value_part, 'tensor', axis=1, tiled=True)  41.5 us
    all_gather x1, blocking collectives, shards(): lax.all_gather(key_part, 'tensor', axis=1, tiled=True)  38.9 us
    all_gather x1, waiting for transfers between devices, shards(): full_rows = lax.all_gather(state_shard, 'tensor', axis=1, tiled=True)  37.2 us
    all_to_all x1, waiting for transfers between devices, shards(): lax.all_to_all(chosen, 'tensor', split_axis=2, concat_axis=1, tiled=True)  17.5 us
  transfers between devices with their start and end apart: 7, of which 6 were waited for; matrix products, arithmetic and copies ran while one was open for 2% of the time, Pallas kernels for 0%

commit v1 on v0

--- a/solution.py
+++ b/solution.py
@@ -79,7 +79,10 @@
         np.arange(tp_count)[:, None] * heads_here // group_size + np.arange(kv_here)[None, :]
     ).reshape(-1)
     routed = jnp.take(suffix_states, request_order, axis=0)
-    routed_here = lax.all_to_all(routed, "dp", split_axis=0, concat_axis=1, tiled=True)
+    routed_here = jnp.concatenate(
+        lax.all_to_all(jnp.stack(jnp.split(routed, lax.axis_size("dp"), axis=0)), "dp", 0, 0),
+        axis=1,
+    )
     width_here = routed_here.shape[2]
     state_shard = routed_here.reshape(row_count, width_here)
     slot_ids = dp_index * local_reqs + jnp.arange(local_reqs, dtype=jnp.int32)

time: 636 us -> 638 us (level)
  transfers between devices with their start and end apart: 7 -> 7, of which waited for: 6 -> 6; matrix products, arithmetic and copies ran while one was open for 2% -> 1% of each run, Pallas kernels for 0% -> 0%
where the time goes in v1:
time: 638 us; the launch traced here: 637 us
  waiting for transfers between devices  422 us (66%)
  blocking collectives  129 us (20%)
  starting transfers between devices  33 us (5%)
  between operations  18.2 us (3%)
  local copies, waits for them, and re-layouts  14.4 us (2%)
  matrix products  11 us (2%)
  other arithmetic  9.54 us (1%)
    reduce_scatter x1, waiting for transfers between devices, shards(): lax.psum_scatter(down_terms.astype(jnp.bfloat16), 'tensor', scatter_dimen...  149 us
    reduce_scatter x1, waiting for transfers between devices, shards(): lax.psum_scatter(attn_terms.astype(jnp.bfloat16), 'tensor', scatter_dimen...  147 us
    all_gather x1, waiting for transfers between devices, shards(): middle_rows = lax.all_gather(middle, 'tensor', axis=1, tiled=True)  59.4 us
    all_gather x1, blocking collectives, shards(): all_rows = lax.all_gather(prefix_cache, 'dp', axis=0, tiled=True)  49 us
    all_gather x1, blocking collectives, shards(): lax.all_gather(value_part, 'tensor', axis=1, tiled=True)  41.6 us
    all_gather x1, blocking collectives, shards(): lax.all_gather(key_part, 'tensor', axis=1, tiled=True)  38.9 us
    all_gather x1, waiting for transfers between devices, shards(): full_rows = lax.all_gather(state_shard, 'tensor', axis=1, tiled=True)  37.3 us
    all_to_all x1, waiting for transfers between devices, shards(): lax.all_to_all(chosen, 'tensor', split_axis=2, concat_axis=1, tiled=True)  19.6 us
  transfers between devices with their start and end apart: 7, of which 6 were waited for; matrix products, arithmetic and copies ran while one was open for 1% of the time, Pallas kernels for 0%

profile of v1, /device:TPU:8, one launch (start us, length us, event | category | flops | bytes accessed | tf_op | source)
XLA Modules:
  0.0 637.5 jit_solution(942688094595153524)
XLA Ops:
  7.2 0.7 compare_select_fusion.3
  8.0 0.7 compare_and_fusion.1
  8.6 1.3 gather_fusion.3
  10.0 1.3 gather_fusion.5
  11.3 0.6 gather_fusion.4
  11.9 0.6 gather_fusion
  12.5 0.1 broadcast_select_fusion
  12.8 0.7 reshape.706
  13.6 16.0 %all-to-all-start = ((bf16[16,2,512]{2,1,0:T(2,128)(2,1)}), bf16[16,2,512]{2,1,0:T(2,128)(2,1)S(1)}, u32[]{:S(2)}, u32[]{:S(2)}) async-start(bf16[16,2,512]{2,1,0:T(2,128)(2,1)} %reshape.706), calls=%async_computation | async-start | bytes 65536 | tf_op jit(solution)/shard_map/all_to_all | solution.py:83
  29.6 49.0 %all_gather.16 = bf16[16,8,1024]{2,1,0:T(8,128)(2,1)S(1)} all-gather(bf16[1,8,1024]{2,1,0:T(8,128)(2,1)S(1)} %copy-done.10), channel_id=1, replica_groups=mesh['dp'=16,'tensor'=32] {'dp'}, dimensions={0}, use_global_device_ids=true | all-gather | bytes 278528 | tf_op jit(solution)/shard_map/all_gather | solution.py:150
  78.5 1.9 gather_fusion.1
  80.4 6.7 %all-to-all-start.1 = ((bf16[16,8,32,128]{3,1,0,2:T(8,128)(2,1)}), bf16[16,8,32,128]{3,1,0,2:T(8,128)(2,1)S(1)}, u32[]{:S(2)}, u32[]{:S(2)}) async-start(bf16[16,8,32,128]{3,1,0,2:T(8,128)(2,1)} %bitcast.23), calls=%async_computation.1 | async-start | bytes 2097152 | tf_op jit(solution)/shard_map/all_to_all | solution.py:153
  87.2 0.1 reshape.707
  87.3 0.7 copy.51
  88.1 0.6 gather_fusion.2
  88.7 0.6 fusion.81
  93.3 0.6 fusion.80
  93.9 0.6 iota_compare_fusion.2
  94.5 0.7 iota_compare_fusion.1
  95.2 0.2 multiply_cosine_fusion
  95.4 19.6 %all-to-all-done.1 = bf16[16,8,32,128]{3,1,0,2:T(8,128)(2,1)S(1)} async-done(((bf16[16,8,32,128]{3,1,0,2:T(8,128)(2,1)}), bf16[16,8,32,128]{3,1,0,2:T(8,128)(2,1)S(1)}, u32[]{:S(2)}, u32[]{:S(2)}) %all-to-all-start.1) | async-done | bytes 1048608 | tf_op jit(solution)/shard_map/all_to_all | solution.py:153
  114.9 0.3 copy_bitcast_fusion
  115.3 0.1 copy.54
  115.4 0.1 copy.57
  115.5 37.3 %all-gather.3.cloned.1.call-done = bf16[256,2048]{0,1:T(8,128)(2,1)} async-done(((bf16[256,64]{0,1:T(8,128)(2,1)}), bf16[256,2048]{0,1:T(8,128)(2,1)}) %all-gather.3.cloned.1.call-update) | async-done | bytes 1048592 | tf_op jit(solution)/shard_map/all_gather | solution.py:95
  152.7 1.6 fusion
  154.4 0.5 convolution_bitcast_fusion
  154.9 0.2 fusion.42
  155.1 0.1 copy-done.15
  155.2 0.5 convolution_convert_fusion.2
  155.7 41.6 %all_gather.18 = bf16[256,512]{0,1:T(8,128)(2,1)S(1)} all-gather(bf16[256,16]{0,1:T(8,128)(2,1)S(1)} %convolution_convert_fusion.2), channel_id=1, replica_groups=mesh['dp'=16,'tensor'=32] {'tensor'}, dimensions={1}, use_global_device_ids=true | all-gather | bytes 270336 | tf_op jit(solution)/shard_map/all_gather | solution.py:107
  197.3 0.5 convolution_convert_fusion.3
  197.8 38.9 %all_gather.17 = bf16[256,512]{0,1:T(8,128)(2,1)S(1)} all-gather(bf16[256,16]{0,1:T(8,128)(2,1)S(1)} %convolution_convert_fusion.3), channel_id=1, replica_groups=mesh['dp'=16,'tensor'=32] {'tensor'}, dimensions={1}, use_global_device_ids=true | all-gather | bytes 270336 | tf_op jit(solution)/shard_map/all_gather | solution.py:106
  236.7 0.2 copy.71
  236.9 0.3 fusion.82
  237.2 0.3 fusion.83
  237.6 0.2 select_reduce_fusion.1
  237.8 0.2 select_reduce_fusion
  238.1 0.1 fusion.35
  238.2 0.2 fusion.25
  238.4 0.2 fusion.9
  238.6 0.1 fusion.33
  238.8 0.2 fusion.23
  239.0 0.2 fusion.10
  239.2 0.2 fusion.12
  239.4 0.2 fusion.11
  239.6 1.5 convolution_convert_fusion.1
  241.2 147.0 %reduce-scatter.3.cloned.1.call-done = bf16[256,64]{0,1:T(8,128)(2,1)} async-done(((bf16[256,2048]{0,1:T(8,128)(2,1)}), bf16[256,64]{0,1:T(8,128)(2,1)}) %reduce-scatter.3.cloned.1.call-update) | async-done | bytes 32784 | tf_op jit(solution)/shard_map/reduce_scatter | solution.py:187
  388.2 1.4 add_convert_fusion
  389.7 59.4 %all-gather.5.cloned.1.call-done = bf16[256,2048]{0,1:T(8,128)(2,1)} async-done(((bf16[256,64]{0,1:T(8,128)(2,1)}), bf16[256,2048]{0,1:T(8,128)(2,1)}) %all-gather.5.cloned.1.call-update) | async-done | bytes 1048592 | tf_op jit(solution)/shard_map/all_gather | solution.py:191
  449.2 1.6 fusion.3
  450.8 2.1 fusion.15
  452.9 4.1 convolution_convert_fusion
  457.1 148.6 %reduce-scatter.5.cloned.1.call-done = bf16[256,64]{0,1:T(8,128)(2,1)} async-done(((bf16[256,2048]{0,1:T(8,128)(2,1)}), bf16[256,64]{0,1:T(8,128)(2,1)}) %reduce-scatter.5.cloned.1.call-update) | async-done | bytes 32784 | tf_op jit(solution)/shard_map/reduce_scatter | solution.py:197
  605.6 0.8 select_convert_fusion
  606.4 0.1 copy.58
  606.6 0.7 reshape.708
  607.3 10.2 %all-to-all-start.2 = ((bf16[16,2,512]{2,1,0:T(2,128)(2,1)}), bf16[16,2,512]{2,1,0:T(2,128)(2,1)S(1)}, u32[]{:S(2)}, u32[]{:S(2)}) async-start(bf16[16,2,512]{2,1,0:T(2,128)(2,1)} %reshape.708), calls=%async_computation.4 | async-start | bytes 65536 | tf_op jit(solution)/shard_map/all_to_all | solution.py:206
  617.5 0.6 copy.73
  618.1 0.6 copy.74
  618.7 9.9 %all-to-all-done.2 = bf16[16,2,512]{2,1,0:T(2,128)(2,1)S(1)} async-done(((bf16[16,2,512]{2,1,0:T(2,128)(2,1)}), bf16[16,2,512]{2,1,0:T(2,128)(2,1)S(1)}, u32[]{:S(2)}, u32[]{:S(2)}) %all-to-all-start.2) | async-done | bytes 32800 | tf_op jit(solution)/shard_map/all_to_all | solution.py:206
  628.6 0.1 reshape.709
  628.8 1.5 scatter_fusion
  630.3 0.6 copy-done.7
  (87 shorter events, 0.9 us)
Async XLA Ops:
  7.2 445.7 %copy-start = (bf16[256,2048]{1,0:T(8,128)(2,1)S(1)}, bf16[256,2048]{1,0:T(8,128)(2,1)}, u32[]{:S(2)}) copy-start(bf16[256,2048]{1,0:T(8,128)(2,1)} %param.39) | copy-start | bytes 3145732
  7.2 4.1 copy-start.1
  7.2 4.7 copy-start.9
  8.6 20.9 %copy-start.10 = (bf16[1,8,1024]{2,1,0:T(8,128)(2,1)S(1)}, bf16[1,8,1024]{2,1,0:T(8,128)(2,1)}, u32[]{:S(2)}) copy-start(bf16[1,8,1024]{2,1,0:T(8,128)(2,1)} %param.30) | copy-start | bytes 49156
  9.9 68.6 %copy-start.13 = (s32[32]{0:T(128)S(1)}, s32[32]{0:T(128)}, u32[]{:S(2)}) copy-start(s32[32]{0:T(128)} %constant.238) | copy-start | bytes 388
  13.6 66.9 %all-to-all-start = ((bf16[16,2,512]{2,1,0:T(2,128)(2,1)}), bf16[16,2,512]{2,1,0:T(2,128)(2,1)S(1)}, u32[]{:S(2)}, u32[]{:S(2)}) async-start(bf16[16,2,512]{2,1,0:T(2,128)(2,1)} %reshape.706), calls=%async_computation | async-start | bytes 65536 | tf_op jit(solution)/shard_map/all_to_all | solution.py:83
  80.4 7.7 %copy-start.2 = (s32[16]{0:T(128)S(1)}, s32[16]{0:T(128)}, u32[]{:S(2)}) copy-start(s32[16]{0:T(128)} %param.28) | copy-start | bytes 196
  80.4 11.5 %copy-start.11 = (bf16[2048]{0:T(1024)(128)(2,1)S(1)}, bf16[2048]{0:T(1024)(128)(2,1)}, u32[]{:S(2)}) copy-start(bf16[2048]{0:T(1024)(128)(2,1)} %param.31) | copy-start | bytes 12292
  80.4 34.5 %all-to-all-start.1 = ((bf16[16,8,32,128]{3,1,0,2:T(8,128)(2,1)}), bf16[16,8,32,128]{3,1,0,2:T(8,128)(2,1)S(1)}, u32[]{:S(2)}, u32[]{:S(2)}) async-start(bf16[16,8,32,128]{3,1,0,2:T(8,128)(2,1)} %bitcast.23), calls=%async_computation.1 | async-start | bytes 2097152 | tf_op jit(solution)/shard_map/all_to_all | solution.py:153
  87.1 65.6 %all-gather.3.cloned.1.call-start = ((), (), s32[]{:S(2)}) async-start(), calls=%async_computation.5 | async-start | bytes 1081344 | tf_op jit(solution)/shard_map/all_gather | solution.py:95
  88.0 300.2 %reduce-scatter.3.cloned.1.call-start = ((), (), s32[]{:S(2)}) async-start(), calls=%async_computation.6 | async-start | bytes 1081344 | tf_op jit(solution)/shard_map/reduce_scatter | solution.py:187
  115.2 39.2 %copy-start.14 = (bf16[2048,64]{0,1:T(8,128)(2,1)S(1)}, bf16[2048,64]{0,1:T(8,128)(2,1)}, u32[]{:S(2)}) copy-start(bf16[2048,64]{0,1:T(8,128)(2,1)} %param.32) | copy-start | bytes 786436
  152.7 1.6 copy-start.3
  154.4 0.8 copy-start.15
  155.2 42.1 %copy-start.16 = (bf16[2048,16]{0,1:T(8,128)(2,1)S(1)}, bf16[2048,16]{0,1:T(8,128)(2,1)}, u32[]{:S(2)}) copy-start(bf16[2048,16]{0,1:T(8,128)(2,1)} %param.33) | copy-start | bytes 196612
  237.6 2.1 copy-start.8
  239.6 148.6 %copy-start.5 = (bf16[256,64]{0,1:T(8,128)(2,1)S(1)}, bf16[256,64]{0,1:T(8,128)(2,1)}, u32[]{:S(2)}) copy-start(bf16[256,64]{0,1:T(8,128)(2,1)} %copy.51) | copy-start | bytes 98308
  239.6 150.1 %copy-start.12 = (bf16[2048]{0:T(1024)(128)(2,1)S(1)}, bf16[2048]{0:T(1024)(128)(2,1)}, u32[]{:S(2)}) copy-start(bf16[2048]{0:T(1024)(128)(2,1)} %param.36) | copy-start | bytes 12292
  241.1 208.0 %all-gather.5.cloned.1.call-start = ((), (), s32[]{:S(2)}) async-start(), calls=%async_computation.7 | async-start | bytes 1081344 | tf_op jit(solution)/shard_map/all_gather | solution.py:191
  389.6 216.0 %reduce-scatter.5.cloned.1.call-start = ((), (), s32[]{:S(2)}) async-start(), calls=%async_computation.8 | async-start | bytes 1081344 | tf_op jit(solution)/shard_map/reduce_scatter | solution.py:197
  449.2 1.6 copy-start.4
  457.0 148.7 %copy-start.6 = (bf16[256,64]{0,1:T(8,128)(2,1)S(1)}, bf16[256,64]{0,1:T(8,128)(2,1)}, u32[]{:S(2)}) copy-start(bf16[256,64]{0,1:T(8,128)(2,1)} %add_convert_fusion) | copy-start | bytes 98308
  607.3 21.3 %all-to-all-start.2 = ((bf16[16,2,512]{2,1,0:T(2,128)(2,1)}), bf16[16,2,512]{2,1,0:T(2,128)(2,1)S(1)}, u32[]{:S(2)}, u32[]{:S(2)}) async-start(bf16[16,2,512]{2,1,0:T(2,128)(2,1)} %reshape.708), calls=%async_computation.4 | async-start | bytes 65536 | tf_op jit(solution)/shard_map/all_to_all | solution.py:206
  630.3 0.6 copy-start.7
Sparse Core Ops, SparseCore 0:
  90.6 62.0 all-gather.2
  241.3 146.9 reduce-scatter.2
  391.0 58.1 all-gather.4
  457.1 148.4 reduce-scatter.4
